TPU v7x, 32 devices: a whole 2x2x4 slice. The times are simulated.
32 devices in a mesh: dp: 8 (over y, x, core), ctx: 4 (over z).
Axes of the slice: x: 2, y: 2, z: 4, core: 2. Of those that a mesh axis runs over, the one named last changes fastest.
Arguments:
- inputs: bfloat16 [16, 1024, 768], P('dp', 'ctx'), may hold values from -6 to 6
- lengths: int32 [16], P('dp'), may hold values from 921 to 1024, as said below
- ln1_gain: bfloat16 [768], P(('dp', 'ctx')), may hold values from 0.5 to 1.5
- ln1_bias: bfloat16 [768], P(('dp', 'ctx')), may hold values from -4 to 4
- query_weight: bfloat16 [768, 768], P(('dp', 'ctx')), may hold values from -0.3125 to 0.3125
- query_bias: bfloat16 [768], P(('dp', 'ctx')), may hold values from -4 to 4
- key_weight: bfloat16 [768, 768], P(('dp', 'ctx')), may hold values from -0.3125 to 0.3125
- value_weight: bfloat16 [768, 768], P(('dp', 'ctx')), may hold values from -0.21875 to 0.21875
- value_bias: bfloat16 [768], P(('dp', 'ctx')), may hold values from -0.75 to 0.75
- out_weight: bfloat16 [768, 768], P(('dp', 'ctx')), may hold values from -1.75 to 1.75
- out_bias: bfloat16 [768], P(('dp', 'ctx')), may hold values from -4 to 4
- ln2_gain: bfloat16 [768], P(('dp', 'ctx')), may hold values from 0.5 to 1.5
- ln2_bias: bfloat16 [768], P(('dp', 'ctx')), may hold values from -4 to 4
- ffn_in_weight: bfloat16 [768, 3072], P(('dp', 'ctx')), may hold values from -0.21875 to 0.21875
- ffn_in_bias: bfloat16 [3072], P(('dp', 'ctx')), may hold values from -4 to 4
- ffn_out_weight: bfloat16 [3072, 768], P(('dp', 'ctx')), may hold values from -0.15625 to 0.15625
- ffn_out_bias: bfloat16 [768], P(('dp', 'ctx')), may hold values from -4 to 4
- out_grad: bfloat16 [16, 1024, 768], P('dp', 'ctx'), may hold values from -6 to 6
Outputs:
- output: bfloat16 [16, 1024, 768], P('dp', 'ctx')
- input_grad: bfloat16 [16, 1024, 768], P('dp', 'ctx')
- grad_ln1_gain: float32 [768], P(('dp', 'ctx'))
- grad_ln1_bias: float32 [768], P(('dp', 'ctx'))
- grad_query: float32 [768, 768], P(('dp', 'ctx'))
- grad_query_bias: float32 [768], P(('dp', 'ctx'))
- grad_key: float32 [768, 768], P(('dp', 'ctx'))
- grad_value: float32 [768, 768], P(('dp', 'ctx'))
- grad_value_bias: float32 [768], P(('dp', 'ctx'))
- grad_out: float32 [768, 768], P(('dp', 'ctx'))
- grad_out_bias: float32 [768], P(('dp', 'ctx'))
- grad_ln2_gain: float32 [768], P(('dp', 'ctx'))
- grad_ln2_bias: float32 [768], P(('dp', 'ctx'))
- grad_ffn_in: float32 [768, 3072], P(('dp', 'ctx'))
- grad_ffn_in_bias: float32 [3072], P(('dp', 'ctx'))
- grad_ffn_out: float32 [3072, 768], P(('dp', 'ctx'))
- grad_ffn_out_bias: float32 [768], P(('dp', 'ctx'))
Inputs may be any that keep to these rules, and one draw needn't show every extreme that they name: `lengths`: A sequence's molecules occupy positions 0 to its length - 1; some sequence has exactly 1024, some exactly 921.
All inputs are finite; a program needn't handle non-finite values.
Results may differ from a plain program's by a relative error of at most 0.015.
Values may be sent and summed in bfloat16 or wider, within the bound.
No kernel may reach another device: no remote copies, remote signals or barrier semaphores. Data moves between devices by JAX's collectives and lax.ppermute only.
A program may use at most 192 MiB of HBM per device.

v0:
```python
import jax
import jax.numpy as jnp
from jax import lax
from jax.sharding import PartitionSpec as P

H = 12
HD = 64


def layer_norm(tok_rows, gain, shift):
    center = tok_rows - jnp.mean(tok_rows, axis=-1, keepdims=True)
    spread = jnp.mean(center * center, axis=-1, keepdims=True)
    return center * lax.rsqrt(spread + 1e-06) * gain + shift


def gelu_exact(values):
    return jax.nn.gelu(values, approximate=False)


def outer_product(left_rows, right_rows):
    return lax.dot_general(
        left_rows, right_rows, (((0,), (0,)), ((), ())), preferred_element_type=jnp.float32
    )


def back_product(grad_rows, weight):
    return lax.dot_general(
        grad_rows, weight, (((1,), (1,)), ((), ())), preferred_element_type=jnp.float32
    )


def column_sum(grad_rows):
    return jnp.sum(grad_rows.astype(jnp.float32), axis=0)


def fetch(shards):
    return (
        lax.all_gather(shards[0], ("dp", "ctx"), axis=0, tiled=True),
        lax.all_gather(shards[1], ("dp", "ctx"), axis=0, tiled=True),
        lax.all_gather(shards[2], ("dp", "ctx"), axis=0, tiled=True),
        lax.all_gather(shards[3], ("dp", "ctx"), axis=0, tiled=True),
        lax.all_gather(shards[4], ("dp", "ctx"), axis=0, tiled=True),
        lax.all_gather(shards[5], ("dp", "ctx"), axis=0, tiled=True),
        lax.all_gather(shards[6], ("dp", "ctx"), axis=0, tiled=True),
        lax.all_gather(shards[7], ("dp", "ctx"), axis=0, tiled=True),
        lax.all_gather(shards[8], ("dp", "ctx"), axis=0, tiled=True),
        lax.all_gather(shards[9], ("dp", "ctx"), axis=0, tiled=True),
        lax.all_gather(shards[10], ("dp", "ctx"), axis=0, tiled=True),
        lax.all_gather(shards[11], ("dp", "ctx"), axis=0, tiled=True),
        lax.all_gather(shards[12], ("dp", "ctx"), axis=0, tiled=True),
        lax.all_gather(shards[13], ("dp", "ctx"), axis=0, tiled=True),
        lax.all_gather(shards[14], ("dp", "ctx"), axis=0, tiled=True),
    )


def forward(tok_block, length, full_set):
    (
        ln1_gain,
        ln1_bias,
        query_weight,
        query_bias,
        key_weight,
        value_weight,
        value_bias,
        out_weight,
        out_bias,
        ln2_gain,
        ln2_bias,
        ffn_in_weight,
        ffn_in_bias,
        ffn_out_weight,
        ffn_out_bias,
    ) = full_set
    seq_rows = tok_block.shape[0]
    tok_rows = tok_block.astype(jnp.float32)
    normed = layer_norm(
        tok_rows, ln1_gain.astype(jnp.float32), ln1_bias.astype(jnp.float32)
    ).astype(jnp.bfloat16)
    queries = (
        jnp.dot(normed, query_weight, preferred_element_type=jnp.float32)
        + query_bias.astype(jnp.float32)
    ).astype(jnp.bfloat16)
    key_rows = jnp.dot(normed, key_weight, preferred_element_type=jnp.float32).astype(jnp.bfloat16)
    value_rows = (
        jnp.dot(normed, value_weight, preferred_element_type=jnp.float32)
        + value_bias.astype(jnp.float32)
    ).astype(jnp.bfloat16)
    all_keys, all_values = (
        lax.all_gather(key_rows, "ctx", axis=0, tiled=True),
        lax.all_gather(value_rows, "ctx", axis=0, tiled=True),
    )
    total_rows = all_keys.shape[0]
    query_heads = queries.reshape(seq_rows, H, HD)
    key_heads = all_keys.reshape(total_rows, H, HD)
    value_heads = all_values.reshape(total_rows, H, HD)
    scores = jnp.einsum(
        "qhd,khd->hqk", query_heads, key_heads, preferred_element_type=jnp.float32
    ) * HD ** (-0.5)
    valid = jnp.arange(total_rows) < length
    scores = jnp.where(valid[None, None, :], scores, -1e30)
    log_total = jax.nn.logsumexp(scores, axis=-1)
    attn_probs = jax.nn.softmax(scores, axis=-1)
    low_probs = attn_probs.astype(jnp.bfloat16)
    mixed_rows = jnp.einsum(
        "hqk,khd->qhd", low_probs, value_heads, preferred_element_type=jnp.float32
    )
    mixed_rows = mixed_rows.reshape(seq_rows, H * HD).astype(jnp.bfloat16)
    middle = (
        tok_rows
        + jnp.dot(mixed_rows, out_weight, preferred_element_type=jnp.float32)
        + out_bias.astype(jnp.float32)
    )
    normed_two = layer_norm(
        middle, ln2_gain.astype(jnp.float32), ln2_bias.astype(jnp.float32)
    ).astype(jnp.bfloat16)
    ffn_pre = jnp.dot(
        normed_two, ffn_in_weight, preferred_element_type=jnp.float32
    ) + ffn_in_bias.astype(jnp.float32)
    ffn_act = gelu_exact(ffn_pre).astype(jnp.bfloat16)
    result = (
        middle
        + jnp.dot(ffn_act, ffn_out_weight, preferred_element_type=jnp.float32)
        + ffn_out_bias.astype(jnp.float32)
    )
    kept = (
        tok_rows,
        normed,
        query_heads,
        key_heads,
        value_heads,
        attn_probs,
        low_probs,
        mixed_rows,
        middle,
        normed_two,
        ffn_pre,
        ffn_act,
        log_total,
        length,
    )
    return (result.astype(jnp.bfloat16), kept)


def backward(kept, cot_block, full_set):
    (
        ln1_gain,
        ln1_bias,
        query_weight,
        query_bias,
        key_weight,
        value_weight,
        value_bias,
        out_weight,
        out_bias,
        ln2_gain,
        ln2_bias,
        ffn_in_weight,
        ffn_in_bias,
        ffn_out_weight,
        ffn_out_bias,
    ) = full_set
    (
        tok_rows,
        normed,
        query_heads,
        key_heads,
        value_heads,
        attn_probs,
        low_probs,
        mixed_rows,
        middle,
        normed_two,
        ffn_pre,
        ffn_act,
        log_total,
        length,
    ) = kept
    seq_rows = tok_rows.shape[0]
    total_rows = key_heads.shape[0]
    score_scale = HD ** (-0.5)
    d_out = cot_block.astype(jnp.float32)
    d_ffn_out = d_out.astype(jnp.bfloat16)
    grad_ffn_out_bias = column_sum(d_ffn_out)
    grad_ffn_out = outer_product(ffn_act, d_ffn_out)
    d_act = back_product(d_ffn_out, ffn_out_weight)
    unused, gelu_back = jax.vjp(gelu_exact, ffn_pre)
    d_pre = gelu_back(d_act)[0].astype(jnp.bfloat16)
    grad_ffn_in_bias = column_sum(d_pre)
    grad_ffn_in = outer_product(normed_two, d_pre)
    d_normed_two = back_product(d_pre, ffn_in_weight)
    unused, second_back = jax.vjp(
        layer_norm, middle, ln2_gain.astype(jnp.float32), ln2_bias.astype(jnp.float32)
    )
    d_middle, grad_ln2_gain, grad_ln2_bias = second_back(d_normed_two)
    d_middle = d_middle + d_out
    d_branch = d_middle.astype(jnp.bfloat16)
    grad_out_bias = column_sum(d_branch)
    grad_out = outer_product(mixed_rows, d_branch)
    d_mixed = back_product(d_branch, out_weight).astype(jnp.bfloat16).reshape(seq_rows, H, HD)
    d_probs = jnp.einsum("qhd,khd->hqk", d_mixed, value_heads, preferred_element_type=jnp.float32)
    row_inner = jnp.sum(attn_probs * d_probs, axis=-1, keepdims=True)
    d_scores = (attn_probs * (d_probs - row_inner)).astype(jnp.bfloat16)
    d_query = (
        jnp.einsum("hqk,khd->qhd", d_scores, key_heads, preferred_element_type=jnp.float32)
        * score_scale
    )
    d_query = d_query.reshape(seq_rows, H * HD).astype(jnp.bfloat16)
    key_terms = (
        jnp.einsum("hqk,qhd->khd", d_scores, query_heads, preferred_element_type=jnp.float32)
        * score_scale
    )
    value_terms = jnp.einsum("hqk,qhd->khd", low_probs, d_mixed, preferred_element_type=jnp.float32)
    key_sums, value_sums = (
        lax.psum_scatter(
            key_terms.reshape(total_rows, H * HD).astype(jnp.bfloat16),
            "ctx",
            scatter_dimension=0,
            tiled=True,
        ).astype(jnp.float32),
        lax.psum_scatter(
            value_terms.reshape(total_rows, H * HD).astype(jnp.bfloat16),
            "ctx",
            scatter_dimension=0,
            tiled=True,
        ).astype(jnp.float32),
    )
    d_key = key_sums.astype(jnp.bfloat16)
    d_value = value_sums.astype(jnp.bfloat16)
    grad_query_bias = column_sum(d_query)
    grad_value_bias = column_sum(d_value)
    grad_query = outer_product(normed, d_query)
    grad_key = outer_product(normed, d_key)
    grad_value = outer_product(normed, d_value)
    d_normed = (
        back_product(d_query, query_weight)
        + back_product(d_key, key_weight)
        + back_product(d_value, value_weight)
    )
    unused, first_back = jax.vjp(
        layer_norm, tok_rows, ln1_gain.astype(jnp.float32), ln1_bias.astype(jnp.float32)
    )
    d_rows, grad_ln1_gain, grad_ln1_bias = first_back(d_normed)
    d_input = (d_middle + d_rows).astype(jnp.bfloat16)
    grads = (
        grad_ln1_gain,
        grad_ln1_bias,
        grad_query,
        grad_query_bias,
        grad_key,
        grad_value,
        grad_value_bias,
        grad_out,
        grad_out_bias,
        grad_ln2_gain,
        grad_ln2_bias,
        grad_ffn_in,
        grad_ffn_in_bias,
        grad_ffn_out,
        grad_ffn_out_bias,
    )
    return (d_input, grads)


def per_device(
    inputs,
    lengths,
    ln1_gain,
    ln1_bias,
    query_weight,
    query_bias,
    key_weight,
    value_weight,
    value_bias,
    out_weight,
    out_bias,
    ln2_gain,
    ln2_bias,
    ffn_in_weight,
    ffn_in_bias,
    ffn_out_weight,
    ffn_out_bias,
    out_grad,
):
    shards = (
        ln1_gain,
        ln1_bias,
        query_weight,
        query_bias,
        key_weight,
        value_weight,
        value_bias,
        out_weight,
        out_bias,
        ln2_gain,
        ln2_bias,
        ffn_in_weight,
        ffn_in_bias,
        ffn_out_weight,
        ffn_out_bias,
    )

    def forward_step(counter, seq_entry):
        tok_block, length = seq_entry
        result, kept = forward(tok_block, length, fetch(shards))
        return (counter, result)

    counter, output = lax.scan(forward_step, jnp.zeros((), jnp.int32), (inputs, lengths))

    def backward_step(totals, seq_entry):
        tok_block, length, cot_block = seq_entry
        full_set = fetch(shards)
        unused, kept = forward(tok_block, length, full_set)
        d_input, grads = backward(kept, cot_block, full_set)
        return (jax.tree.map(jnp.add, totals, grads), d_input)

    groups = lax.axis_size(("dp", "ctx"))
    start_totals = tuple(
        (
            jnp.zeros((shard_item.shape[0] * groups,) + shard_item.shape[1:], jnp.float32)
            for shard_item in shards
        )
    )
    totals, input_grad = lax.scan(backward_step, start_totals, (inputs, lengths, out_grad))
    grad_shards = lax.psum_scatter(totals, ("dp", "ctx"), scatter_dimension=0, tiled=True)
    return (output, input_grad) + tuple(grad_shards)


def solution(mesh):
    return jax.shard_map(
        per_device,
        mesh=mesh,
        in_specs=(
            P("dp", "ctx", None),
            P("dp"),
            P(("dp", "ctx")),
            P(("dp", "ctx")),
            P(("dp", "ctx"), None),
            P(("dp", "ctx")),
            P(("dp", "ctx"), None),
            P(("dp", "ctx"), None),
            P(("dp", "ctx")),
            P(("dp", "ctx"), None),
            P(("dp", "ctx")),
            P(("dp", "ctx")),
            P(("dp", "ctx")),
            P(("dp", "ctx"), None),
            P(("dp", "ctx")),
            P(("dp", "ctx"), None),
            P(("dp", "ctx")),
            P("dp", "ctx", None),
        ),
        out_specs=(
            P("dp", "ctx", None),
            P("dp", "ctx", None),
            P(("dp", "ctx")),
            P(("dp", "ctx")),
            P(("dp", "ctx"), None),
            P(("dp", "ctx")),
            P(("dp", "ctx"), None),
            P(("dp", "ctx"), None),
            P(("dp", "ctx")),
            P(("dp", "ctx"), None),
            P(("dp", "ctx")),
            P(("dp", "ctx")),
            P(("dp", "ctx")),
            P(("dp", "ctx"), None),
            P(("dp", "ctx")),
            P(("dp", "ctx"), None),
            P(("dp", "ctx")),
        ),
        check_vma=False,
    )
```

profile of v0, /device:TPU:0, one launch (start us, length us, event | category | flops | bytes accessed | tf_op | source)
XLA Modules:
  0.0 2723.2 jit_solution(3749500177245971645)
XLA Ops:
  8.2 888.4 %while.51 = (s32[]{:T(128)}, bf16[2,256,768]{2,1,0:T(8,128)(2,1)S(1)}, bf16[2,256,768]{2,1,0:T(8,128)(2,1)}, bf16[24]{0:T(256)(128)(2,1)}, bf16[24]{0:T(256)(128...) while((s32[]{:T(128)}, ...), condition=%wide.region_7.8_spmd, body=%wide.region_0.7_spmd.sunk | while | flops 4508832256 | bytes 116793320 | solution.py:307
  18.1 42.5 %all-reduce.39 = (bf16[768]{0:T(1024)(128)(2,1)S(1)}, bf16[768]{0:T(1024)(128)(2,1)S(1)}, bf16[768]{0:T(1024)(128)(2,1)S(1)}, bf16[768]{0:T(1024)(128)(2,1)S(1)}...) all-reduce(bf16[768]{0:T(1024)(128)(2,1)S(1)} %dynamic-update-slice, ...), channel_id=1, replica_groups=mesh['dp'=8,'ctx'=4] {'dp','ctx'}, use_global_device_ids=true, to_apply=%add.2 | all-reduce | flops 9216 | bytes 36864 | tf_op jit(solution)/shard_map/while
  71.7 52.9 %all-gather.17.cloned.1.call-done = bf16[768,768]{1,0:T(8,128)(2,1)} async-done(((bf16[24,768]{1,0:T(8,128)(2,1)}), bf16[768,768]{1,0:T(8,128)(2,1)}) %all-gather.17.cloned.1.call-update) | async-done | bytes 1179664 | tf_op jit(solution)/shard_map/while/body/eval_jaxpr/all_gather | solution.py:43
  132.9 47.5 %all-gather.21.cloned.1.call-done = bf16[768,768]{1,0:T(8,128)(2,1)} async-done(((bf16[24,768]{1,0:T(8,128)(2,1)}), bf16[768,768]{1,0:T(8,128)(2,1)}) %all-gather.21.cloned.1.call-update) | async-done | bytes 1179664 | tf_op jit(solution)/shard_map/while/body/eval_jaxpr/all_gather | solution.py:40
  182.3 36.0 %all-gather.25.cloned.1.call-done = bf16[1024,768]{1,0:T(8,128)(2,1)} async-done(((bf16[256,768]{1,0:T(8,128)(2,1)}), bf16[1024,768]{1,0:T(8,128)(2,1)}) %all-gather.25.cloned.1.call-update) | async-done | bytes 1572880 | tf_op jit(solution)/shard_map/while/body/eval_jaxpr/all_gather | solution.py:89
  220.0 36.2 %all-gather.19.cloned.1.call-done = bf16[1024,768]{1,0:T(8,128)(2,1)} async-done(((bf16[256,768]{1,0:T(8,128)(2,1)}), bf16[1024,768]{1,0:T(8,128)(2,1)}) %all-gather.19.cloned.1.call-update) | async-done | bytes 1572880 | tf_op jit(solution)/shard_map/while/body/eval_jaxpr/all_gather | solution.py:90
  274.2 37.6 %all-gather.27.cloned.1.call-done = bf16[768,768]{1,0:T(8,128)(2,1)} async-done(((bf16[24,768]{1,0:T(8,128)(2,1)}), bf16[768,768]{1,0:T(8,128)(2,1)}) %all-gather.27.cloned.1.call-update) | async-done | bytes 1179664 | tf_op jit(solution)/shard_map/while/body/eval_jaxpr/all_gather | solution.py:45
  313.9 63.2 %all-gather.29.cloned.1.call-done = bf16[3072,768]{1,0:T(8,128)(2,1)} async-done(((bf16[96,768]{1,0:T(8,128)(2,1)}), bf16[3072,768]{1,0:T(8,128)(2,1)}) %all-gather.29.cloned.1.call-update) | async-done | bytes 4718608 | tf_op jit(solution)/shard_map/while/body/eval_jaxpr/all_gather | solution.py:51
  377.1 64.7 %all-gather.31.cloned.1.call-done = bf16[768,3072]{1,0:T(8,128)(2,1)} async-done(((bf16[24,3072]{1,0:T(8,128)(2,1)}), bf16[768,3072]{1,0:T(8,128)(2,1)}) %all-gather.31.cloned.1.call-update) | async-done | bytes 4718608 | tf_op jit(solution)/shard_map/while/body/eval_jaxpr/all_gather | solution.py:49
  441.9 12.9 fusion.316
  464.4 39.8 %all-reduce.39 = (bf16[768]{0:T(1024)(128)(2,1)S(1)}, bf16[768]{0:T(1024)(128)(2,1)S(1)}, bf16[768]{0:T(1024)(128)(2,1)S(1)}, bf16[768]{0:T(1024)(128)(2,1)S(1)}...) all-reduce(bf16[768]{0:T(1024)(128)(2,1)S(1)} %dynamic-update-slice, ...), channel_id=1, replica_groups=mesh['dp'=8,'ctx'=4] {'dp','ctx'}, use_global_device_ids=true, to_apply=%add.2 | all-reduce | flops 9216 | bytes 36864 | tf_op jit(solution)/shard_map/while
  513.7 52.9 %all-gather.17.cloned.1.call-done = bf16[768,768]{1,0:T(8,128)(2,1)} async-done(((bf16[24,768]{1,0:T(8,128)(2,1)}), bf16[768,768]{1,0:T(8,128)(2,1)}) %all-gather.17.cloned.1.call-update) | async-done | bytes 1179664 | tf_op jit(solution)/shard_map/while/body/eval_jaxpr/all_gather | solution.py:43
  574.6 47.8 %all-gather.21.cloned.1.call-done = bf16[768,768]{1,0:T(8,128)(2,1)} async-done(((bf16[24,768]{1,0:T(8,128)(2,1)}), bf16[768,768]{1,0:T(8,128)(2,1)}) %all-gather.21.cloned.1.call-update) | async-done | bytes 1179664 | tf_op jit(solution)/shard_map/while/body/eval_jaxpr/all_gather | solution.py:40
  624.4 36.0 %all-gather.25.cloned.1.call-done = bf16[1024,768]{1,0:T(8,128)(2,1)} async-done(((bf16[256,768]{1,0:T(8,128)(2,1)}), bf16[1024,768]{1,0:T(8,128)(2,1)}) %all-gather.25.cloned.1.call-update) | async-done | bytes 1572880 | tf_op jit(solution)/shard_map/while/body/eval_jaxpr/all_gather | solution.py:89
  662.1 36.3 %all-gather.19.cloned.1.call-done = bf16[1024,768]{1,0:T(8,128)(2,1)} async-done(((bf16[256,768]{1,0:T(8,128)(2,1)}), bf16[1024,768]{1,0:T(8,128)(2,1)}) %all-gather.19.cloned.1.call-update) | async-done | bytes 1572880 | tf_op jit(solution)/shard_map/while/body/eval_jaxpr/all_gather | solution.py:90
  716.4 37.6 %all-gather.27.cloned.1.call-done = bf16[768,768]{1,0:T(8,128)(2,1)} async-done(((bf16[24,768]{1,0:T(8,128)(2,1)}), bf16[768,768]{1,0:T(8,128)(2,1)}) %all-gather.27.cloned.1.call-update) | async-done | bytes 1179664 | tf_op jit(solution)/shard_map/while/body/eval_jaxpr/all_gather | solution.py:45
  756.1 63.1 %all-gather.29.cloned.1.call-done = bf16[3072,768]{1,0:T(8,128)(2,1)} async-done(((bf16[96,768]{1,0:T(8,128)(2,1)}), bf16[3072,768]{1,0:T(8,128)(2,1)}) %all-gather.29.cloned.1.call-update) | async-done | bytes 4718608 | tf_op jit(solution)/shard_map/while/body/eval_jaxpr/all_gather | solution.py:51
  819.2 64.6 %all-gather.31.cloned.1.call-done = bf16[768,3072]{1,0:T(8,128)(2,1)} async-done(((bf16[24,3072]{1,0:T(8,128)(2,1)}), bf16[768,3072]{1,0:T(8,128)(2,1)}) %all-gather.31.cloned.1.call-update) | async-done | bytes 4718608 | tf_op jit(solution)/shard_map/while/body/eval_jaxpr/all_gather | solution.py:49
  883.8 12.9 fusion.316
  897.8 1116.4 %while.52 = (s32[]{:T(128)}, f32[768]{0:T(1024)}, f32[768]{0:T(1024)}, f32[768,768]{1,0:T(8,128)}, f32[768]{0:T(1024)}, /*index=5*/f32[768,768]{1,0:T(8,128)}, f...) while((s32[]{:T(128)}, f32[768]{0:T(1024)}, ...), condition=%wide.region_31.32_spmd.clone, body=%wide.region_8.31_spmd.clone.sunk | while | flops 12278196224 | bytes 516163296 | solution.py:323
  930.1 39.5 %all-reduce.40 = (bf16[768]{0:T(1024)(128)(2,1)S(1)}, bf16[768]{0:T(1024)(128)(2,1)S(1)}, bf16[3072]{0:T(1024)(128)(2,1)S(1)}, bf16[768]{0:T(1024)(128)(2,1)S(1)...) all-reduce(bf16[768]{0:T(1024)(128)(2,1)S(1)} %dynamic-update-slice, ...), channel_id=1, replica_groups=mesh['dp'=8,'ctx'=4] {'dp','ctx'}, use_global_device_ids=true, to_apply=%add.10 | all-reduce | flops 8448 | bytes 33792 | tf_op jit(solution)/shard_map/while
  980.1 52.9 %all-gather.33.cloned.1.call-done = bf16[768,768]{1,0:T(8,128)(2,1)} async-done(((bf16[24,768]{1,0:T(8,128)(2,1)}), bf16[768,768]{1,0:T(8,128)(2,1)}) %all-gather.33.cloned.1.call-update) | async-done | bytes 1179664 | tf_op jit(solution)/shard_map/while/body/eval_jaxpr/all_gather | solution.py:42
  1039.0 49.7 %all-gather.37.cloned.1.call-done = bf16[768,768]{1,0:T(8,128)(2,1)} async-done(((bf16[24,768]{1,0:T(8,128)(2,1)}), bf16[768,768]{1,0:T(8,128)(2,1)}) %all-gather.37.cloned.1.call-update) | async-done | bytes 1179664 | tf_op jit(solution)/shard_map/while/body/eval_jaxpr/all_gather | solution.py:40
  1090.7 35.4 %all-gather.41.cloned.1.call-done = bf16[1024,768]{1,0:T(8,128)(2,1)} async-done(((bf16[256,768]{1,0:T(8,128)(2,1)}), bf16[1024,768]{1,0:T(8,128)(2,1)}) %all-gather.41.cloned.1.call-update) | async-done | bytes 1572880 | tf_op jit(solution)/shard_map/while/body/eval_jaxpr/all_gather | solution.py:90
  1128.7 34.9 %all-gather.35.cloned.1.call-done = bf16[1024,768]{1,0:T(8,128)(2,1)} async-done(((bf16[256,768]{1,0:T(8,128)(2,1)}), bf16[1024,768]{1,0:T(8,128)(2,1)}) %all-gather.35.cloned.1.call-update) | async-done | bytes 1572880 | tf_op jit(solution)/shard_map/while/body/eval_jaxpr/all_gather | solution.py:89
  1179.5 39.8 %all-gather.43.cloned.1.call-done = bf16[768,768]{1,0:T(8,128)(2,1)} async-done(((bf16[24,768]{1,0:T(8,128)(2,1)}), bf16[768,768]{1,0:T(8,128)(2,1)}) %all-gather.43.cloned.1.call-update) | async-done | bytes 1179664 | tf_op jit(solution)/shard_map/while/body/eval_jaxpr/all_gather | solution.py:45
  1221.4 63.2 %all-gather.45.cloned.1.call-done = bf16[768,3072]{1,0:T(8,128)(2,1)} async-done(((bf16[24,3072]{1,0:T(8,128)(2,1)}), bf16[768,3072]{1,0:T(8,128)(2,1)}) %all-gather.45.cloned.1.call-update) | async-done | bytes 4718608 | tf_op jit(solution)/shard_map/while/body/eval_jaxpr/all_gather | solution.py:49
  1290.1 59.1 %all-gather.47.cloned.1.call-done = bf16[3072,768]{1,0:T(8,128)(2,1)} async-done(((bf16[96,768]{1,0:T(8,128)(2,1)}), bf16[3072,768]{1,0:T(8,128)(2,1)}) %all-gather.47.cloned.1.call-update) | async-done | bytes 4718608 | tf_op jit(solution)/shard_map/while/body/eval_jaxpr/all_gather | solution.py:51
  1349.2 11.1 convert_reduce_fusion.15
  1431.0 28.6 %reduce-scatter.23.cloned.1.call-done = bf16[256,768]{0,1:T(8,128)(2,1)} async-done(((bf16[1024,768]{0,1:T(8,128)(2,1)}), bf16[256,768]{0,1:T(8,128)(2,1)}) %reduce-scatter.23.cloned.1.call-update) | async-done | bytes 393232 | tf_op jit(solution)/shard_map/while/body/eval_jaxpr/reduce_scatter | solution.py:220
  1476.3 39.7 %all-reduce.40 = (bf16[768]{0:T(1024)(128)(2,1)S(1)}, bf16[768]{0:T(1024)(128)(2,1)S(1)}, bf16[3072]{0:T(1024)(128)(2,1)S(1)}, bf16[768]{0:T(1024)(128)(2,1)S(1)...) all-reduce(bf16[768]{0:T(1024)(128)(2,1)S(1)} %dynamic-update-slice, ...), channel_id=1, replica_groups=mesh['dp'=8,'ctx'=4] {'dp','ctx'}, use_global_device_ids=true, to_apply=%add.10 | all-reduce | flops 8448 | bytes 33792 | tf_op jit(solution)/shard_map/while
  1526.7 53.0 %all-gather.33.cloned.1.call-done = bf16[768,768]{1,0:T(8,128)(2,1)} async-done(((bf16[24,768]{1,0:T(8,128)(2,1)}), bf16[768,768]{1,0:T(8,128)(2,1)}) %all-gather.33.cloned.1.call-update) | async-done | bytes 1179664 | tf_op jit(solution)/shard_map/while/body/eval_jaxpr/all_gather | solution.py:42
  1585.7 49.7 %all-gather.37.cloned.1.call-done = bf16[768,768]{1,0:T(8,128)(2,1)} async-done(((bf16[24,768]{1,0:T(8,128)(2,1)}), bf16[768,768]{1,0:T(8,128)(2,1)}) %all-gather.37.cloned.1.call-update) | async-done | bytes 1179664 | tf_op jit(solution)/shard_map/while/body/eval_jaxpr/all_gather | solution.py:40
  1637.4 35.4 %all-gather.41.cloned.1.call-done = bf16[1024,768]{1,0:T(8,128)(2,1)} async-done(((bf16[256,768]{1,0:T(8,128)(2,1)}), bf16[1024,768]{1,0:T(8,128)(2,1)}) %all-gather.41.cloned.1.call-update) | async-done | bytes 1572880 | tf_op jit(solution)/shard_map/while/body/eval_jaxpr/all_gather | solution.py:90
  1675.4 34.9 %all-gather.35.cloned.1.call-done = bf16[1024,768]{1,0:T(8,128)(2,1)} async-done(((bf16[256,768]{1,0:T(8,128)(2,1)}), bf16[1024,768]{1,0:T(8,128)(2,1)}) %all-gather.35.cloned.1.call-update) | async-done | bytes 1572880 | tf_op jit(solution)/shard_map/while/body/eval_jaxpr/all_gather | solution.py:89
  1726.2 39.8 %all-gather.43.cloned.1.call-done = bf16[768,768]{1,0:T(8,128)(2,1)} async-done(((bf16[24,768]{1,0:T(8,128)(2,1)}), bf16[768,768]{1,0:T(8,128)(2,1)}) %all-gather.43.cloned.1.call-update) | async-done | bytes 1179664 | tf_op jit(solution)/shard_map/while/body/eval_jaxpr/all_gather | solution.py:45
  1768.1 63.1 %all-gather.45.cloned.1.call-done = bf16[768,3072]{1,0:T(8,128)(2,1)} async-done(((bf16[24,3072]{1,0:T(8,128)(2,1)}), bf16[768,3072]{1,0:T(8,128)(2,1)}) %all-gather.45.cloned.1.call-update) | async-done | bytes 4718608 | tf_op jit(solution)/shard_map/while/body/eval_jaxpr/all_gather | solution.py:49
  1836.7 59.3 %all-gather.47.cloned.1.call-done = bf16[3072,768]{1,0:T(8,128)(2,1)} async-done(((bf16[96,768]{1,0:T(8,128)(2,1)}), bf16[3072,768]{1,0:T(8,128)(2,1)}) %all-gather.47.cloned.1.call-update) | async-done | bytes 4718608 | tf_op jit(solution)/shard_map/while/body/eval_jaxpr/all_gather | solution.py:51
  1895.9 11.1 convert_reduce_fusion.15
  1970.9 12.1 select_add_fusion.38
  1985.0 21.3 reduce-scatter.23.cloned.1.call-done
  2018.2 40.0 %all-reduce.36 = (f32[768]{0:T(1024)S(1)}, f32[768]{0:T(1024)S(1)}, f32[768]{0:T(1024)S(1)}, f32[768]{0:T(1024)S(1)}, f32[768]{0:T(1024)S(1)}, /*index=5*/f32[76...) all-reduce(f32[768]{0:T(1024)S(1)} %copy-done.57, ...), channel_id=4, replica_groups=mesh['dp'=8,'ctx'=4] {'dp','ctx'}, use_global_device_ids=true, to_apply=%region_32.33.clone | all-reduce | flops 9216 | bytes 73728
  2063.5 55.5 %reduce-scatter.9.cloned.1.call-done = f32[24,768]{1,0:T(8,128)} async-done(((f32[768,768]{1,0:T(8,128)}), f32[24,768]{1,0:T(8,128)}) %reduce-scatter.9.cloned.1.call-update) | async-done | bytes 73744 | tf_op jit(solution)/shard_map/reduce_scatter | solution.py:324
  2119.1 104.4 %reduce-scatter.11.cloned.1.call-done = f32[24,768]{1,0:T(8,128)} async-done(((f32[768,768]{1,0:T(8,128)}), f32[24,768]{1,0:T(8,128)}) %reduce-scatter.11.cloned.1.call-update) | async-done | bytes 73744 | tf_op jit(solution)/shard_map/reduce_scatter | solution.py:324
  2223.5 104.3 %reduce-scatter.13.cloned.1.call-done = f32[24,768]{1,0:T(8,128)} async-done(((f32[768,768]{1,0:T(8,128)}), f32[24,768]{1,0:T(8,128)}) %reduce-scatter.13.cloned.1.call-update) | async-done | bytes 73744 | tf_op jit(solution)/shard_map/reduce_scatter | solution.py:324
  2327.8 104.5 %reduce-scatter.15.cloned.1.call-done = f32[24,768]{1,0:T(8,128)} async-done(((f32[768,768]{1,0:T(8,128)}), f32[24,768]{1,0:T(8,128)}) %reduce-scatter.15.cloned.1.call-update) | async-done | bytes 73744 | tf_op jit(solution)/shard_map/reduce_scatter | solution.py:324
  2432.3 141.7 %reduce-scatter.17.cloned.1.call-done = f32[24,3072]{1,0:T(8,128)} async-done(((f32[768,3072]{1,0:T(8,128)}), f32[24,3072]{1,0:T(8,128)}) %reduce-scatter.17.cloned.1.call-update) | async-done | bytes 294928 | tf_op jit(solution)/shard_map/reduce_scatter | solution.py:324
  2574.0 141.7 %reduce-scatter.19.cloned.1.call-done = f32[96,768]{1,0:T(8,128)} async-done(((f32[3072,768]{1,0:T(8,128)}), f32[96,768]{1,0:T(8,128)}) %reduce-scatter.19.cloned.1.call-update) | async-done | bytes 294928 | tf_op jit(solution)/shard_map/reduce_scatter | solution.py:324
  (623 shorter events, 371.3 us)
Async XLA Ops:
  8.2 60.6 %all-gather.23.cloned.1.call-start = ((), (), s32[]{:S(2)}) async-start(), calls=%async_computation.17 | async-start | bytes 1216512 | tf_op jit(solution)/shard_map/while/body/eval_jaxpr/all_gather | solution.py:42
  9.0 115.6 %all-gather.17.cloned.1.call-start = ((), (), s32[]{:S(2)}) async-start(), calls=%async_computation.14 | async-start | bytes 1216512 | tf_op jit(solution)/shard_map/while/body/eval_jaxpr/all_gather | solution.py:43
  9.7 170.6 %all-gather.21.cloned.1.call-start = ((), (), s32[]{:S(2)}) async-start(), calls=%async_computation.16 | async-start | bytes 1216512 | tf_op jit(solution)/shard_map/while/body/eval_jaxpr/all_gather | solution.py:40
  10.5 207.8 %all-gather.25.cloned.1.call-start = ((), (), s32[]{:S(2)}) async-start(), calls=%async_computation.18 | async-start | bytes 1966080 | tf_op jit(solution)/shard_map/while/body/eval_jaxpr/all_gather | solution.py:89
  71.6 184.6 %all-gather.19.cloned.1.call-start = ((), (), s32[]{:S(2)}) async-start(), calls=%async_computation.15 | async-start | bytes 1966080 | tf_op jit(solution)/shard_map/while/body/eval_jaxpr/all_gather | solution.py:90
  127.2 184.6 %all-gather.27.cloned.1.call-start = ((), (), s32[]{:S(2)}) async-start(), calls=%async_computation.19 | async-start | bytes 1216512 | tf_op jit(solution)/shard_map/while/body/eval_jaxpr/all_gather | solution.py:45
  127.8 249.4 %all-gather.29.cloned.1.call-start = ((), (), s32[]{:S(2)}) async-start(), calls=%async_computation.20 | async-start | bytes 4866048 | tf_op jit(solution)/shard_map/while/body/eval_jaxpr/all_gather | solution.py:51
  128.5 313.3 %all-gather.31.cloned.1.call-start = ((), (), s32[]{:S(2)}) async-start(), calls=%async_computation.21 | async-start | bytes 4866048 | tf_op jit(solution)/shard_map/while/body/eval_jaxpr/all_gather | solution.py:49
  274.2 167.7 %copy-start.60 = (f32[768]{0:T(1024)S(1)}, f32[768]{0:T(1024)}, u32[]{:S(2)}) copy-start(f32[768]{0:T(1024)} %convert_element_type.492) | copy-start | bytes 9220 | tf_op jit(solution)/shard_map/while
  274.2 167.7 %copy-start.61 = (f32[768]{0:T(1024)S(1)}, f32[768]{0:T(1024)}, u32[]{:S(2)}) copy-start(f32[768]{0:T(1024)} %convert_element_type.493) | copy-start | bytes 9220 | tf_op jit(solution)/shard_map/while
  274.2 167.7 %copy-start.62 = (f32[768]{0:T(1024)S(1)}, f32[768]{0:T(1024)}, u32[]{:S(2)}) copy-start(f32[768]{0:T(1024)} %convert_element_type.494) | copy-start | bytes 9220 | tf_op jit(solution)/shard_map/while
  454.8 56.2 %all-gather.23.cloned.1.call-start = ((), (), s32[]{:S(2)}) async-start(), calls=%async_computation.17 | async-start | bytes 1216512 | tf_op jit(solution)/shard_map/while/body/eval_jaxpr/all_gather | solution.py:42
  455.5 111.1 %all-gather.17.cloned.1.call-start = ((), (), s32[]{:S(2)}) async-start(), calls=%async_computation.14 | async-start | bytes 1216512 | tf_op jit(solution)/shard_map/while/body/eval_jaxpr/all_gather | solution.py:43
  456.1 166.3 %all-gather.21.cloned.1.call-start = ((), (), s32[]{:S(2)}) async-start(), calls=%async_computation.16 | async-start | bytes 1216512 | tf_op jit(solution)/shard_map/while/body/eval_jaxpr/all_gather | solution.py:40
  456.8 203.5 %all-gather.25.cloned.1.call-start = ((), (), s32[]{:S(2)}) async-start(), calls=%async_computation.18 | async-start | bytes 1966080 | tf_op jit(solution)/shard_map/while/body/eval_jaxpr/all_gather | solution.py:89
  513.7 184.7 %all-gather.19.cloned.1.call-start = ((), (), s32[]{:S(2)}) async-start(), calls=%async_computation.15 | async-start | bytes 1966080 | tf_op jit(solution)/shard_map/while/body/eval_jaxpr/all_gather | solution.py:90
  569.2 184.7 %all-gather.27.cloned.1.call-start = ((), (), s32[]{:S(2)}) async-start(), calls=%async_computation.19 | async-start | bytes 1216512 | tf_op jit(solution)/shard_map/while/body/eval_jaxpr/all_gather | solution.py:45
  569.8 249.4 %all-gather.29.cloned.1.call-start = ((), (), s32[]{:S(2)}) async-start(), calls=%async_computation.20 | async-start | bytes 4866048 | tf_op jit(solution)/shard_map/while/body/eval_jaxpr/all_gather | solution.py:51
  570.4 313.4 %all-gather.31.cloned.1.call-start = ((), (), s32[]{:S(2)}) async-start(), calls=%async_computation.21 | async-start | bytes 4866048 | tf_op jit(solution)/shard_map/while/body/eval_jaxpr/all_gather | solution.py:49
  716.4 167.4 %copy-start.60 = (f32[768]{0:T(1024)S(1)}, f32[768]{0:T(1024)}, u32[]{:S(2)}) copy-start(f32[768]{0:T(1024)} %convert_element_type.492) | copy-start | bytes 9220 | tf_op jit(solution)/shard_map/while
  716.4 167.4 %copy-start.61 = (f32[768]{0:T(1024)S(1)}, f32[768]{0:T(1024)}, u32[]{:S(2)}) copy-start(f32[768]{0:T(1024)} %convert_element_type.493) | copy-start | bytes 9220 | tf_op jit(solution)/shard_map/while
  716.4 167.4 %copy-start.62 = (f32[768]{0:T(1024)S(1)}, f32[768]{0:T(1024)}, u32[]{:S(2)}) copy-start(f32[768]{0:T(1024)} %convert_element_type.494) | copy-start | bytes 9220 | tf_op jit(solution)/shard_map/while
  921.4 56.0 %all-gather.39.cloned.1.call-start = ((), (), s32[]{:S(2)}) async-start(), calls=%async_computation.25 | async-start | bytes 1216512 | tf_op jit(solution)/shard_map/while/body/eval_jaxpr/all_gather | solution.py:43
  921.9 111.0 %all-gather.33.cloned.1.call-start = ((), (), s32[]{:S(2)}) async-start(), calls=%async_computation.22 | async-start | bytes 1216512 | tf_op jit(solution)/shard_map/while/body/eval_jaxpr/all_gather | solution.py:42
  922.5 166.2 %all-gather.37.cloned.1.call-start = ((), (), s32[]{:S(2)}) async-start(), calls=%async_computation.24 | async-start | bytes 1216512 | tf_op jit(solution)/shard_map/while/body/eval_jaxpr/all_gather | solution.py:40
  923.3 202.8 %all-gather.41.cloned.1.call-start = ((), (), s32[]{:S(2)}) async-start(), calls=%async_computation.26 | async-start | bytes 1966080 | tf_op jit(solution)/shard_map/while/body/eval_jaxpr/all_gather | solution.py:90
  980.0 183.5 %all-gather.35.cloned.1.call-start = ((), (), s32[]{:S(2)}) async-start(), calls=%async_computation.23 | async-start | bytes 1966080 | tf_op jit(solution)/shard_map/while/body/eval_jaxpr/all_gather | solution.py:89
  1035.6 183.7 %all-gather.43.cloned.1.call-start = ((), (), s32[]{:S(2)}) async-start(), calls=%async_computation.27 | async-start | bytes 1216512 | tf_op jit(solution)/shard_map/while/body/eval_jaxpr/all_gather | solution.py:45
  1036.3 248.3 %all-gather.45.cloned.1.call-start = ((), (), s32[]{:S(2)}) async-start(), calls=%async_computation.28 | async-start | bytes 4866048 | tf_op jit(solution)/shard_map/while/body/eval_jaxpr/all_gather | solution.py:49
  1037.0 312.2 %all-gather.47.cloned.1.call-start = ((), (), s32[]{:S(2)}) async-start(), calls=%async_computation.29 | async-start | bytes 4866048 | tf_op jit(solution)/shard_map/while/body/eval_jaxpr/all_gather | solution.py:51
  1037.6 391.2 %reduce-scatter.21.cloned.1.call-start = ((), (), s32[]{:S(2)}) async-start(), calls=%async_computation.30 | async-start | bytes 1966080 | tf_op jit(solution)/shard_map/while/body/eval_jaxpr/reduce_scatter | solution.py:214
  1389.1 70.4 %reduce-scatter.23.cloned.1.call-start = ((), (), s32[]{:S(2)}) async-start(), calls=%async_computation.31 | async-start | bytes 1966080 | tf_op jit(solution)/shard_map/while/body/eval_jaxpr/reduce_scatter | solution.py:220
  1467.5 56.4 %all-gather.39.cloned.1.call-start = ((), (), s32[]{:S(2)}) async-start(), calls=%async_computation.25 | async-start | bytes 1216512 | tf_op jit(solution)/shard_map/while/body/eval_jaxpr/all_gather | solution.py:43
  1468.1 111.6 %all-gather.33.cloned.1.call-start = ((), (), s32[]{:S(2)}) async-start(), calls=%async_computation.22 | async-start | bytes 1216512 | tf_op jit(solution)/shard_map/while/body/eval_jaxpr/all_gather | solution.py:42
  1468.8 166.6 %all-gather.37.cloned.1.call-start = ((), (), s32[]{:S(2)}) async-start(), calls=%async_computation.24 | async-start | bytes 1216512 | tf_op jit(solution)/shard_map/while/body/eval_jaxpr/all_gather | solution.py:40
  1469.6 203.2 %all-gather.41.cloned.1.call-start = ((), (), s32[]{:S(2)}) async-start(), calls=%async_computation.26 | async-start | bytes 1966080 | tf_op jit(solution)/shard_map/while/body/eval_jaxpr/all_gather | solution.py:90
  1526.6 183.7 %all-gather.35.cloned.1.call-start = ((), (), s32[]{:S(2)}) async-start(), calls=%async_computation.23 | async-start | bytes 1966080 | tf_op jit(solution)/shard_map/while/body/eval_jaxpr/all_gather | solution.py:89
  1582.3 183.7 %all-gather.43.cloned.1.call-start = ((), (), s32[]{:S(2)}) async-start(), calls=%async_computation.27 | async-start | bytes 1216512 | tf_op jit(solution)/shard_map/while/body/eval_jaxpr/all_gather | solution.py:45
  1583.0 248.2 %all-gather.45.cloned.1.call-start = ((), (), s32[]{:S(2)}) async-start(), calls=%async_computation.28 | async-start | bytes 4866048 | tf_op jit(solution)/shard_map/while/body/eval_jaxpr/all_gather | solution.py:49
  1583.6 312.3 %all-gather.47.cloned.1.call-start = ((), (), s32[]{:S(2)}) async-start(), calls=%async_computation.29 | async-start | bytes 4866048 | tf_op jit(solution)/shard_map/while/body/eval_jaxpr/all_gather | solution.py:51
  1584.3 398.7 %reduce-scatter.21.cloned.1.call-start = ((), (), s32[]{:S(2)}) async-start(), calls=%async_computation.30 | async-start | bytes 1966080 | tf_op jit(solution)/shard_map/while/body/eval_jaxpr/reduce_scatter | solution.py:214
  1935.8 70.4 %reduce-scatter.23.cloned.1.call-start = ((), (), s32[]{:S(2)}) async-start(), calls=%async_computation.31 | async-start | bytes 1966080 | tf_op jit(solution)/shard_map/while/body/eval_jaxpr/reduce_scatter | solution.py:220
  2014.2 104.9 %reduce-scatter.9.cloned.1.call-start = ((), (), s32[]{:S(2)}) async-start(), calls=%async_computation.8 | async-start | bytes 2433024 | tf_op jit(solution)/shard_map/reduce_scatter | solution.py:324
  2014.8 208.7 %reduce-scatter.11.cloned.1.call-start = ((), (), s32[]{:S(2)}) async-start(), calls=%async_computation.9 | async-start | bytes 2433024 | tf_op jit(solution)/shard_map/reduce_scatter | solution.py:324
  2015.4 312.4 %reduce-scatter.13.cloned.1.call-start = ((), (), s32[]{:S(2)}) async-start(), calls=%async_computation.10 | async-start | bytes 2433024 | tf_op jit(solution)/shard_map/reduce_scatter | solution.py:324
  2015.9 416.3 %reduce-scatter.15.cloned.1.call-start = ((), (), s32[]{:S(2)}) async-start(), calls=%async_computation.11 | async-start | bytes 2433024 | tf_op jit(solution)/shard_map/reduce_scatter | solution.py:324
  2016.7 557.3 %reduce-scatter.17.cloned.1.call-start = ((), (), s32[]{:S(2)}) async-start(), calls=%async_computation.12 | async-start | bytes 9732096 | tf_op jit(solution)/shard_map/reduce_scatter | solution.py:324
  2017.4 698.3 %reduce-scatter.19.cloned.1.call-start = ((), (), s32[]{:S(2)}) async-start(), calls=%async_computation.13 | async-start | bytes 9732096 | tf_op jit(solution)/shard_map/reduce_scatter | solution.py:324
  (126 other events, 2823.6 us)
Sparse Core Ops, SparseCore 0:
  11.9 56.9 all-gather.22
  71.7 52.8 all-gather.16
  127.4 52.9 all-gather.20
  182.3 35.9 all-gather.24
  220.3 35.8 all-gather.18
  258.9 52.8 all-gather.26
  314.6 62.5 all-gather.28
  379.9 61.8 all-gather.30
  458.4 52.5 all-gather.22
  513.6 52.9 all-gather.16
  569.4 52.9 all-gather.20
  624.4 35.9 all-gather.24
  662.5 35.8 all-gather.18
  701.1 52.8 all-gather.26
  756.6 62.5 all-gather.28
  821.8 61.8 all-gather.30
  924.7 52.6 all-gather.38
  980.0 52.9 all-gather.32
  1035.7 52.8 all-gather.36
  1090.1 35.9 all-gather.40
  1127.7 35.8 all-gather.34
  1166.4 52.8 all-gather.42
  1222.1 62.5 all-gather.44
  1287.3 61.8 all-gather.46
  1389.2 33.7 reduce-scatter.20
  1425.2 34.3 reduce-scatter.22
  1470.8 53.0 all-gather.38
  1526.7 52.8 all-gather.32
  1582.5 52.9 all-gather.36
  1636.8 35.9 all-gather.40
  1674.4 35.8 all-gather.34
  1713.1 52.8 all-gather.42
  1768.7 62.5 all-gather.44
  1834.0 61.8 all-gather.46
  1935.9 33.7 reduce-scatter.20
  1971.9 34.3 reduce-scatter.22
Sparse Core Ops, SparseCore 1:
  2020.5 98.5 reduce-scatter.8
  2124.8 98.6 reduce-scatter.10
  2229.2 98.5 reduce-scatter.12
  2333.7 98.5 reduce-scatter.14
  2438.8 135.2 reduce-scatter.16
  2580.5 135.2 reduce-scatter.18
where the time goes:
time: 2740 us; the launch traced here: 2720 us
  waiting for transfers between devices  2090 us (76%)
  matrix products  274 us (10%)
  blocking collectives  201 us (7%)
  local copies, waits for them, and re-layouts  77.8 us (3%)
  other arithmetic  38.4 us (1%)
    reduce_scatter x6, waiting for transfers between devices, per_device(): lax.psum_scatter(totals, ('dp', 'ctx'), scatter_dimension=0, tiled=True)  652 us
    all_gather x4, waiting for transfers between devices, fetch(): lax.all_gather(shards[11], ('dp', 'ctx'), axis=0, tiled=True)  256 us
    all_gather x4, waiting for transfers between devices, fetch(): lax.all_gather(shards[13], ('dp', 'ctx'), axis=0, tiled=True)  245 us
    all_gather x4, waiting for transfers between devices, fetch(): lax.all_gather(shards[2], ('dp', 'ctx'), axis=0, tiled=True)  195 us
    while x4, blocking collectives  161 us
    all_gather x4, waiting for transfers between devices, fetch(): lax.all_gather(shards[7], ('dp', 'ctx'), axis=0, tiled=True)  155 us
    all_gather x4, waiting for transfers between devices, forward(): lax.all_gather(value_rows, 'ctx', axis=0, tiled=True)  143 us
    all_gather x4, waiting for transfers between devices, forward(): lax.all_gather(key_rows, 'ctx', axis=0, tiled=True)  142 us
  transfers between devices with their start and end apart: 42, of which 40 were waited for; matrix products, arithmetic and copies ran while one was open for 10% of the time, Pallas kernels for 0%

commit v1 on v0

--- a/solution.py
+++ b/solution.py
@@ -34,10 +34,33 @@
 
 
 def fetch(shards):
+
+    def _part_paths(a0):
+        high, z, newest = (
+            jax.lax.axis_size(("dp", "ctx")),
+            jax.lax.axis_index(("dp", "ctx")),
+            a0.shape[0],
+        )
+        answer, v1 = (a0, 1)
+        while v1 < high:
+            answer = jnp.concatenate(
+                [
+                    answer,
+                    jax.lax.ppermute(
+                        answer,
+                        axis_name=("dp", "ctx"),
+                        perm=[(rr, (rr - v1) % high) for rr in range(high)],
+                    ),
+                ],
+                axis=0,
+            )
+            v1 = 2 * v1
+        return jnp.roll(answer, z * newest, axis=0)
+
     return (
         lax.all_gather(shards[0], ("dp", "ctx"), axis=0, tiled=True),
         lax.all_gather(shards[1], ("dp", "ctx"), axis=0, tiled=True),
-        lax.all_gather(shards[2], ("dp", "ctx"), axis=0, tiled=True),
+        _part_paths(shards[2]),
         lax.all_gather(shards[3], ("dp", "ctx"), axis=0, tiled=True),
         lax.all_gather(shards[4], ("dp", "ctx"), axis=0, tiled=True),
         lax.all_gather(shards[5], ("dp", "ctx"), axis=0, tiled=True),

time: 2740 us -> 2560 us (0.934)
  waiting for transfers between devices: 2090 us -> 1910 us
    all_gather x4 -> x0, waiting for transfers between devices: 195 us -> none  [fetch(): lax.all_gather(shards[2], ('dp', 'ctx'), axis=0, tiled=True)]
    ppermute x0 -> x5, waiting for transfers between devices: none -> 30.7 us  [_part_paths(): jax.lax.ppermute(answer, axis_name=('dp', 'ctx'), perm=[(rr, (rr - v1) %...]
  transfers between devices with their start and end apart: 42 -> 43, of which waited for: 40 -> 41; matrix products, arithmetic and copies ran while one was open for 10% -> 10% of each run, Pallas kernels for 0% -> 0%
where the time goes in v1:
time: 2560 us; the launch traced here: 2550 us
  waiting for transfers between devices  1910 us (75%)
  matrix products  277 us (11%)
  blocking collectives  200 us (8%)
  local copies, waits for them, and re-layouts  80 us (3%)
  other arithmetic  32.2 us (1%)
  loops' own time  27.6 us (1%)
    reduce_scatter x6, waiting for transfers between devices, per_device(): lax.psum_scatter(totals, ('dp', 'ctx'), scatter_dimension=0, tiled=True)  652 us
    all_gather x4, waiting for transfers between devices, fetch(): lax.all_gather(shards[11], ('dp', 'ctx'), axis=0, tiled=True)  256 us
    all_gather x4, waiting for transfers between devices, fetch(): lax.all_gather(shards[13], ('dp', 'ctx'), axis=0, tiled=True)  245 us
    while x4, blocking collectives  160 us
    all_gather x4, waiting for transfers between devices, fetch(): lax.all_gather(shards[7], ('dp', 'ctx'), axis=0, tiled=True)  154 us
    all_gather x4, waiting for transfers between devices, forward(): lax.all_gather(value_rows, 'ctx', axis=0, tiled=True)  128 us
    all_gather x4, waiting for transfers between devices, fetch(): lax.all_gather(shards[4], ('dp', 'ctx'), axis=0, tiled=True)  123 us
    all_gather x4, waiting for transfers between devices, forward(): lax.all_gather(key_rows, 'ctx', axis=0, tiled=True)  123 us
  transfers between devices with their start and end apart: 43, of which 41 were waited for; matrix products, arithmetic and copies ran while one was open for 10% of the time, Pallas kernels for 0%

profile of v1, /device:TPU:0, one launch (start us, length us, event | category | flops | bytes accessed | tf_op | source)
XLA Modules:
  0.0 2547.6 jit_solution(16398912482839072735)
XLA Ops:
  39.4 13.9 collective-permute-done.4
  54.3 776.4 %while.55 = (s32[]{:T(128)}, bf16[2,256,768]{2,1,0:T(8,128)(2,1)S(1)}, bf16[2,256,768]{2,1,0:T(8,128)(2,1)S(1)}, bf16[24]{0:T(256)(128)(2,1)}, bf16[24]{0:T(256)...) while((s32[]{:T(128)}, ...), condition=%wide.region_7.9_spmd, body=%wide.region_0.8_spmd.sunk | while | flops 4511191552 | bytes 110000456 | solution.py:330
  62.7 41.3 %all-reduce.39 = (bf16[768]{0:T(1024)(128)(2,1)S(1)}, bf16[768]{0:T(1024)(128)(2,1)S(1)}, bf16[768]{0:T(1024)(128)(2,1)S(1)}, bf16[768]{0:T(1024)(128)(2,1)S(1)}...) all-reduce(bf16[768]{0:T(1024)(128)(2,1)S(1)} %dynamic-update-slice, ...), channel_id=1, replica_groups=mesh['dp'=8,'ctx'=4] {'dp','ctx'}, use_global_device_ids=true, to_apply=%add.2 | all-reduce | flops 9216 | bytes 36864 | tf_op jit(solution)/shard_map/while
  116.5 53.3 %all-gather.15.cloned.1.call-done = bf16[768,768]{1,0:T(8,128)(2,1)} async-done(((bf16[24,768]{1,0:T(8,128)(2,1)}), bf16[768,768]{1,0:T(8,128)(2,1)}) %all-gather.15.cloned.1.call-update) | async-done | bytes 1179664 | tf_op jit(solution)/shard_map/while/body/eval_jaxpr/all_gather | solution.py:66
  181.4 26.6 %all-gather.21.cloned.1.call-done = bf16[1024,768]{1,0:T(8,128)(2,1)} async-done(((bf16[256,768]{1,0:T(8,128)(2,1)}), bf16[1024,768]{1,0:T(8,128)(2,1)}) %all-gather.21.cloned.1.call-update) | async-done | bytes 1572880 | tf_op jit(solution)/shard_map/while/body/eval_jaxpr/all_gather | solution.py:112
  209.7 36.2 %all-gather.17.cloned.1.call-done = bf16[1024,768]{1,0:T(8,128)(2,1)} async-done(((bf16[256,768]{1,0:T(8,128)(2,1)}), bf16[1024,768]{1,0:T(8,128)(2,1)}) %all-gather.17.cloned.1.call-update) | async-done | bytes 1572880 | tf_op jit(solution)/shard_map/while/body/eval_jaxpr/all_gather | solution.py:113
  264.0 37.4 %all-gather.23.cloned.1.call-done = bf16[768,768]{1,0:T(8,128)(2,1)} async-done(((bf16[24,768]{1,0:T(8,128)(2,1)}), bf16[768,768]{1,0:T(8,128)(2,1)}) %all-gather.23.cloned.1.call-update) | async-done | bytes 1179664 | tf_op jit(solution)/shard_map/while/body/eval_jaxpr/all_gather | solution.py:68
  303.5 63.1 %all-gather.25.cloned.1.call-done = bf16[3072,768]{1,0:T(8,128)(2,1)} async-done(((bf16[96,768]{1,0:T(8,128)(2,1)}), bf16[3072,768]{1,0:T(8,128)(2,1)}) %all-gather.25.cloned.1.call-update) | async-done | bytes 4718608 | tf_op jit(solution)/shard_map/while/body/eval_jaxpr/all_gather | solution.py:74
  366.6 64.7 %all-gather.27.cloned.1.call-done = bf16[768,3072]{1,0:T(8,128)(2,1)} async-done(((bf16[24,3072]{1,0:T(8,128)(2,1)}), bf16[768,3072]{1,0:T(8,128)(2,1)}) %all-gather.27.cloned.1.call-update) | async-done | bytes 4718608 | tf_op jit(solution)/shard_map/while/body/eval_jaxpr/all_gather | solution.py:72
  431.4 12.9 fusion.320
  452.8 39.9 %all-reduce.39 = (bf16[768]{0:T(1024)(128)(2,1)S(1)}, bf16[768]{0:T(1024)(128)(2,1)S(1)}, bf16[768]{0:T(1024)(128)(2,1)S(1)}, bf16[768]{0:T(1024)(128)(2,1)S(1)}...) all-reduce(bf16[768]{0:T(1024)(128)(2,1)S(1)} %dynamic-update-slice, ...), channel_id=1, replica_groups=mesh['dp'=8,'ctx'=4] {'dp','ctx'}, use_global_device_ids=true, to_apply=%add.2 | all-reduce | flops 9216 | bytes 36864 | tf_op jit(solution)/shard_map/while
  503.2 53.0 %all-gather.15.cloned.1.call-done = bf16[768,768]{1,0:T(8,128)(2,1)} async-done(((bf16[24,768]{1,0:T(8,128)(2,1)}), bf16[768,768]{1,0:T(8,128)(2,1)}) %all-gather.15.cloned.1.call-update) | async-done | bytes 1179664 | tf_op jit(solution)/shard_map/while/body/eval_jaxpr/all_gather | solution.py:66
  567.8 26.4 %all-gather.21.cloned.1.call-done = bf16[1024,768]{1,0:T(8,128)(2,1)} async-done(((bf16[256,768]{1,0:T(8,128)(2,1)}), bf16[1024,768]{1,0:T(8,128)(2,1)}) %all-gather.21.cloned.1.call-update) | async-done | bytes 1572880 | tf_op jit(solution)/shard_map/while/body/eval_jaxpr/all_gather | solution.py:112
  595.9 36.4 %all-gather.17.cloned.1.call-done = bf16[1024,768]{1,0:T(8,128)(2,1)} async-done(((bf16[256,768]{1,0:T(8,128)(2,1)}), bf16[1024,768]{1,0:T(8,128)(2,1)}) %all-gather.17.cloned.1.call-update) | async-done | bytes 1572880 | tf_op jit(solution)/shard_map/while/body/eval_jaxpr/all_gather | solution.py:113
  650.4 37.4 %all-gather.23.cloned.1.call-done = bf16[768,768]{1,0:T(8,128)(2,1)} async-done(((bf16[24,768]{1,0:T(8,128)(2,1)}), bf16[768,768]{1,0:T(8,128)(2,1)}) %all-gather.23.cloned.1.call-update) | async-done | bytes 1179664 | tf_op jit(solution)/shard_map/while/body/eval_jaxpr/all_gather | solution.py:68
  689.9 63.2 %all-gather.25.cloned.1.call-done = bf16[3072,768]{1,0:T(8,128)(2,1)} async-done(((bf16[96,768]{1,0:T(8,128)(2,1)}), bf16[3072,768]{1,0:T(8,128)(2,1)}) %all-gather.25.cloned.1.call-update) | async-done | bytes 4718608 | tf_op jit(solution)/shard_map/while/body/eval_jaxpr/all_gather | solution.py:74
  753.2 64.6 %all-gather.27.cloned.1.call-done = bf16[768,3072]{1,0:T(8,128)(2,1)} async-done(((bf16[24,3072]{1,0:T(8,128)(2,1)}), bf16[768,3072]{1,0:T(8,128)(2,1)}) %all-gather.27.cloned.1.call-update) | async-done | bytes 4718608 | tf_op jit(solution)/shard_map/while/body/eval_jaxpr/all_gather | solution.py:72
  817.8 12.9 fusion.320
  831.8 1006.9 %while.56 = (s32[]{:T(128)}, f32[768]{0:T(1024)}, f32[768]{0:T(1024)}, f32[768,768]{1,0:T(8,128)}, f32[768]{0:T(1024)}, /*index=5*/f32[768,768]{1,0:T(8,128)}, f...) while((s32[]{:T(128)}, f32[768]{0:T(1024)}, ...), condition=%wide.region_31.33_spmd.clone, body=%wide.region_8.32_spmd.clone.sunk | while | flops 12282914816 | bytes 534598752 | solution.py:346
  862.5 39.7 %all-reduce.40 = (bf16[768]{0:T(1024)(128)(2,1)S(1)}, bf16[768]{0:T(1024)(128)(2,1)S(1)}, bf16[3072]{0:T(1024)(128)(2,1)S(1)}, bf16[768]{0:T(1024)(128)(2,1)S(1)...) all-reduce(bf16[768]{0:T(1024)(128)(2,1)S(1)} %dynamic-update-slice, ...), channel_id=1, replica_groups=mesh['dp'=8,'ctx'=4] {'dp','ctx'}, use_global_device_ids=true, to_apply=%add.10 | all-reduce | flops 8448 | bytes 33792 | tf_op jit(solution)/shard_map/while
  913.0 53.1 %all-gather.29.cloned.1.call-done = bf16[768,768]{1,0:T(8,128)(2,1)} async-done(((bf16[24,768]{1,0:T(8,128)(2,1)}), bf16[768,768]{1,0:T(8,128)(2,1)}) %all-gather.29.cloned.1.call-update) | async-done | bytes 1179664 | tf_op jit(solution)/shard_map/while/body/eval_jaxpr/all_gather | solution.py:65
  975.5 27.9 %all-gather.35.cloned.1.call-done = bf16[1024,768]{1,0:T(8,128)(2,1)} async-done(((bf16[256,768]{1,0:T(8,128)(2,1)}), bf16[1024,768]{1,0:T(8,128)(2,1)}) %all-gather.35.cloned.1.call-update) | async-done | bytes 1572880 | tf_op jit(solution)/shard_map/while/body/eval_jaxpr/all_gather | solution.py:113
  1006.0 34.8 %all-gather.31.cloned.1.call-done = bf16[1024,768]{1,0:T(8,128)(2,1)} async-done(((bf16[256,768]{1,0:T(8,128)(2,1)}), bf16[1024,768]{1,0:T(8,128)(2,1)}) %all-gather.31.cloned.1.call-update) | async-done | bytes 1572880 | tf_op jit(solution)/shard_map/while/body/eval_jaxpr/all_gather | solution.py:112
  1056.8 39.7 %all-gather.37.cloned.1.call-done = bf16[768,768]{1,0:T(8,128)(2,1)} async-done(((bf16[24,768]{1,0:T(8,128)(2,1)}), bf16[768,768]{1,0:T(8,128)(2,1)}) %all-gather.37.cloned.1.call-update) | async-done | bytes 1179664 | tf_op jit(solution)/shard_map/while/body/eval_jaxpr/all_gather | solution.py:68
  1098.6 63.1 %all-gather.39.cloned.1.call-done = bf16[768,3072]{1,0:T(8,128)(2,1)} async-done(((bf16[24,3072]{1,0:T(8,128)(2,1)}), bf16[768,3072]{1,0:T(8,128)(2,1)}) %all-gather.39.cloned.1.call-update) | async-done | bytes 4718608 | tf_op jit(solution)/shard_map/while/body/eval_jaxpr/all_gather | solution.py:72
  1167.2 59.2 %all-gather.41.cloned.1.call-done = bf16[3072,768]{1,0:T(8,128)(2,1)} async-done(((bf16[96,768]{1,0:T(8,128)(2,1)}), bf16[3072,768]{1,0:T(8,128)(2,1)}) %all-gather.41.cloned.1.call-update) | async-done | bytes 4718608 | tf_op jit(solution)/shard_map/while/body/eval_jaxpr/all_gather | solution.py:74
  1226.4 11.1 convert_reduce_fusion.15
  1244.1 10.9 multiply_reduce_fusion.12
  1293.7 10.0 select_add_fusion.38
  1305.6 31.1 %reduce-scatter.23.cloned.1.call-done = bf16[256,768]{0,1:T(8,128)(2,1)} async-done(((bf16[1024,768]{0,1:T(8,128)(2,1)}), bf16[256,768]{0,1:T(8,128)(2,1)}) %reduce-scatter.23.cloned.1.call-update) | async-done | bytes 393232 | tf_op jit(solution)/shard_map/while/body/eval_jaxpr/reduce_scatter | solution.py:243
  1353.4 39.5 %all-reduce.40 = (bf16[768]{0:T(1024)(128)(2,1)S(1)}, bf16[768]{0:T(1024)(128)(2,1)S(1)}, bf16[3072]{0:T(1024)(128)(2,1)S(1)}, bf16[768]{0:T(1024)(128)(2,1)S(1)...) all-reduce(bf16[768]{0:T(1024)(128)(2,1)S(1)} %dynamic-update-slice, ...), channel_id=1, replica_groups=mesh['dp'=8,'ctx'=4] {'dp','ctx'}, use_global_device_ids=true, to_apply=%add.10 | all-reduce | flops 8448 | bytes 33792 | tf_op jit(solution)/shard_map/while
  1404.4 52.9 %all-gather.29.cloned.1.call-done = bf16[768,768]{1,0:T(8,128)(2,1)} async-done(((bf16[24,768]{1,0:T(8,128)(2,1)}), bf16[768,768]{1,0:T(8,128)(2,1)}) %all-gather.29.cloned.1.call-update) | async-done | bytes 1179664 | tf_op jit(solution)/shard_map/while/body/eval_jaxpr/all_gather | solution.py:65
  1466.7 27.9 %all-gather.35.cloned.1.call-done = bf16[1024,768]{1,0:T(8,128)(2,1)} async-done(((bf16[256,768]{1,0:T(8,128)(2,1)}), bf16[1024,768]{1,0:T(8,128)(2,1)}) %all-gather.35.cloned.1.call-update) | async-done | bytes 1572880 | tf_op jit(solution)/shard_map/while/body/eval_jaxpr/all_gather | solution.py:113
  1497.2 34.8 %all-gather.31.cloned.1.call-done = bf16[1024,768]{1,0:T(8,128)(2,1)} async-done(((bf16[256,768]{1,0:T(8,128)(2,1)}), bf16[1024,768]{1,0:T(8,128)(2,1)}) %all-gather.31.cloned.1.call-update) | async-done | bytes 1572880 | tf_op jit(solution)/shard_map/while/body/eval_jaxpr/all_gather | solution.py:112
  1548.0 39.7 %all-gather.37.cloned.1.call-done = bf16[768,768]{1,0:T(8,128)(2,1)} async-done(((bf16[24,768]{1,0:T(8,128)(2,1)}), bf16[768,768]{1,0:T(8,128)(2,1)}) %all-gather.37.cloned.1.call-update) | async-done | bytes 1179664 | tf_op jit(solution)/shard_map/while/body/eval_jaxpr/all_gather | solution.py:68
  1589.8 63.2 %all-gather.39.cloned.1.call-done = bf16[768,3072]{1,0:T(8,128)(2,1)} async-done(((bf16[24,3072]{1,0:T(8,128)(2,1)}), bf16[768,3072]{1,0:T(8,128)(2,1)}) %all-gather.39.cloned.1.call-update) | async-done | bytes 4718608 | tf_op jit(solution)/shard_map/while/body/eval_jaxpr/all_gather | solution.py:72
  1658.6 59.1 %all-gather.41.cloned.1.call-done = bf16[3072,768]{1,0:T(8,128)(2,1)} async-done(((bf16[96,768]{1,0:T(8,128)(2,1)}), bf16[3072,768]{1,0:T(8,128)(2,1)}) %all-gather.41.cloned.1.call-update) | async-done | bytes 4718608 | tf_op jit(solution)/shard_map/while/body/eval_jaxpr/all_gather | solution.py:74
  1717.6 11.1 convert_reduce_fusion.15
  1735.3 10.9 multiply_reduce_fusion.12
  1789.5 12.2 select_add_fusion.38
  1803.7 24.3 reduce-scatter.23.cloned.1.call-done
  1842.8 39.9 %all-reduce.36 = (f32[768]{0:T(1024)S(1)}, f32[768]{0:T(1024)S(1)}, f32[768]{0:T(1024)S(1)}, f32[768]{0:T(1024)S(1)}, f32[768]{0:T(1024)S(1)}, /*index=5*/f32[76...) all-reduce(f32[768]{0:T(1024)S(1)} %copy-done.64, ...), channel_id=4, replica_groups=mesh['dp'=8,'ctx'=4] {'dp','ctx'}, use_global_device_ids=true, to_apply=%region_32.34.clone | all-reduce | flops 9216 | bytes 73728
  1888.0 55.5 %reduce-scatter.9.cloned.1.call-done = f32[24,768]{1,0:T(8,128)} async-done(((f32[768,768]{1,0:T(8,128)}), f32[24,768]{1,0:T(8,128)}) %reduce-scatter.9.cloned.1.call-update) | async-done | bytes 73744 | tf_op jit(solution)/shard_map/reduce_scatter | solution.py:347
  1943.5 104.4 %reduce-scatter.11.cloned.1.call-done = f32[24,768]{1,0:T(8,128)} async-done(((f32[768,768]{1,0:T(8,128)}), f32[24,768]{1,0:T(8,128)}) %reduce-scatter.11.cloned.1.call-update) | async-done | bytes 73744 | tf_op jit(solution)/shard_map/reduce_scatter | solution.py:347
  2047.9 104.4 %reduce-scatter.13.cloned.1.call-done = f32[24,768]{1,0:T(8,128)} async-done(((f32[768,768]{1,0:T(8,128)}), f32[24,768]{1,0:T(8,128)}) %reduce-scatter.13.cloned.1.call-update) | async-done | bytes 73744 | tf_op jit(solution)/shard_map/reduce_scatter | solution.py:347
  2152.2 104.5 %reduce-scatter.15.cloned.1.call-done = f32[24,768]{1,0:T(8,128)} async-done(((f32[768,768]{1,0:T(8,128)}), f32[24,768]{1,0:T(8,128)}) %reduce-scatter.15.cloned.1.call-update) | async-done | bytes 73744 | tf_op jit(solution)/shard_map/reduce_scatter | solution.py:347
  2256.7 141.8 %reduce-scatter.17.cloned.1.call-done = f32[24,3072]{1,0:T(8,128)} async-done(((f32[768,3072]{1,0:T(8,128)}), f32[24,3072]{1,0:T(8,128)}) %reduce-scatter.17.cloned.1.call-update) | async-done | bytes 294928 | tf_op jit(solution)/shard_map/reduce_scatter | solution.py:347
  2398.5 141.7 %reduce-scatter.19.cloned.1.call-done = f32[96,768]{1,0:T(8,128)} async-done(((f32[3072,768]{1,0:T(8,128)}), f32[96,768]{1,0:T(8,128)}) %reduce-scatter.19.cloned.1.call-update) | async-done | bytes 294928 | tf_op jit(solution)/shard_map/reduce_scatter | solution.py:347
  (664 shorter events, 372.5 us)
Async XLA Ops:
  8.0 8.4 collective-permute-start
  17.2 6.0 collective-permute-start.1
  24.0 2.7 collective-permute-start.2
  27.6 9.6 collective-permute-start.3
  37.9 15.4 collective-permute-start.4
  54.3 59.6 %all-gather.19.cloned.1.call-start = ((), (), s32[]{:S(2)}) async-start(), calls=%async_computation.16 | async-start | bytes 1216512 | tf_op jit(solution)/shard_map/while/body/eval_jaxpr/all_gather | solution.py:65
  55.0 114.8 %all-gather.15.cloned.1.call-start = ((), (), s32[]{:S(2)}) async-start(), calls=%async_computation.14 | async-start | bytes 1216512 | tf_op jit(solution)/shard_map/while/body/eval_jaxpr/all_gather | solution.py:66
  55.8 152.2 %all-gather.21.cloned.1.call-start = ((), (), s32[]{:S(2)}) async-start(), calls=%async_computation.17 | async-start | bytes 1966080 | tf_op jit(solution)/shard_map/while/body/eval_jaxpr/all_gather | solution.py:112
  116.4 129.5 %all-gather.17.cloned.1.call-start = ((), (), s32[]{:S(2)}) async-start(), calls=%async_computation.15 | async-start | bytes 1966080 | tf_op jit(solution)/shard_map/while/body/eval_jaxpr/all_gather | solution.py:113
  172.4 129.0 %all-gather.23.cloned.1.call-start = ((), (), s32[]{:S(2)}) async-start(), calls=%async_computation.18 | async-start | bytes 1216512 | tf_op jit(solution)/shard_map/while/body/eval_jaxpr/all_gather | solution.py:68
  173.0 193.6 %all-gather.25.cloned.1.call-start = ((), (), s32[]{:S(2)}) async-start(), calls=%async_computation.19 | async-start | bytes 4866048 | tf_op jit(solution)/shard_map/while/body/eval_jaxpr/all_gather | solution.py:74
  173.6 257.8 %all-gather.27.cloned.1.call-start = ((), (), s32[]{:S(2)}) async-start(), calls=%async_computation.20 | async-start | bytes 4866048 | tf_op jit(solution)/shard_map/while/body/eval_jaxpr/all_gather | solution.py:72
  264.0 167.4 %copy-start.67 = (f32[768]{0:T(1024)S(1)}, f32[768]{0:T(1024)}, u32[]{:S(2)}) copy-start(f32[768]{0:T(1024)} %convert_element_type.598) | copy-start | bytes 9220 | tf_op jit(solution)/shard_map/while
  264.0 167.4 %copy-start.68 = (f32[768]{0:T(1024)S(1)}, f32[768]{0:T(1024)}, u32[]{:S(2)}) copy-start(f32[768]{0:T(1024)} %convert_element_type.599) | copy-start | bytes 9220 | tf_op jit(solution)/shard_map/while
  444.3 56.3 %all-gather.19.cloned.1.call-start = ((), (), s32[]{:S(2)}) async-start(), calls=%async_computation.16 | async-start | bytes 1216512 | tf_op jit(solution)/shard_map/while/body/eval_jaxpr/all_gather | solution.py:65
  445.0 111.2 %all-gather.15.cloned.1.call-start = ((), (), s32[]{:S(2)}) async-start(), calls=%async_computation.14 | async-start | bytes 1216512 | tf_op jit(solution)/shard_map/while/body/eval_jaxpr/all_gather | solution.py:66
  445.8 148.5 %all-gather.21.cloned.1.call-start = ((), (), s32[]{:S(2)}) async-start(), calls=%async_computation.17 | async-start | bytes 1966080 | tf_op jit(solution)/shard_map/while/body/eval_jaxpr/all_gather | solution.py:112
  503.2 129.1 %all-gather.17.cloned.1.call-start = ((), (), s32[]{:S(2)}) async-start(), calls=%async_computation.15 | async-start | bytes 1966080 | tf_op jit(solution)/shard_map/while/body/eval_jaxpr/all_gather | solution.py:113
  558.8 129.0 %all-gather.23.cloned.1.call-start = ((), (), s32[]{:S(2)}) async-start(), calls=%async_computation.18 | async-start | bytes 1216512 | tf_op jit(solution)/shard_map/while/body/eval_jaxpr/all_gather | solution.py:68
  559.4 193.8 %all-gather.25.cloned.1.call-start = ((), (), s32[]{:S(2)}) async-start(), calls=%async_computation.19 | async-start | bytes 4866048 | tf_op jit(solution)/shard_map/while/body/eval_jaxpr/all_gather | solution.py:74
  560.2 257.6 %all-gather.27.cloned.1.call-start = ((), (), s32[]{:S(2)}) async-start(), calls=%async_computation.20 | async-start | bytes 4866048 | tf_op jit(solution)/shard_map/while/body/eval_jaxpr/all_gather | solution.py:72
  650.4 167.4 %copy-start.67 = (f32[768]{0:T(1024)S(1)}, f32[768]{0:T(1024)}, u32[]{:S(2)}) copy-start(f32[768]{0:T(1024)} %convert_element_type.598) | copy-start | bytes 9220 | tf_op jit(solution)/shard_map/while
  650.4 167.4 %copy-start.68 = (f32[768]{0:T(1024)S(1)}, f32[768]{0:T(1024)}, u32[]{:S(2)}) copy-start(f32[768]{0:T(1024)} %convert_element_type.599) | copy-start | bytes 9220 | tf_op jit(solution)/shard_map/while
  650.4 167.4 %copy-start.69 = (f32[768]{0:T(1024)S(1)}, f32[768]{0:T(1024)}, u32[]{:S(2)}) copy-start(f32[768]{0:T(1024)} %convert_element_type.600) | copy-start | bytes 9220 | tf_op jit(solution)/shard_map/while
  854.5 55.8 %all-gather.33.cloned.1.call-start = ((), (), s32[]{:S(2)}) async-start(), calls=%async_computation.23 | async-start | bytes 1216512 | tf_op jit(solution)/shard_map/while/body/eval_jaxpr/all_gather | solution.py:66
  855.1 110.9 %all-gather.29.cloned.1.call-start = ((), (), s32[]{:S(2)}) async-start(), calls=%async_computation.21 | async-start | bytes 1216512 | tf_op jit(solution)/shard_map/while/body/eval_jaxpr/all_gather | solution.py:65
  855.7 147.7 %all-gather.35.cloned.1.call-start = ((), (), s32[]{:S(2)}) async-start(), calls=%async_computation.24 | async-start | bytes 1966080 | tf_op jit(solution)/shard_map/while/body/eval_jaxpr/all_gather | solution.py:113
  912.9 127.9 %all-gather.31.cloned.1.call-start = ((), (), s32[]{:S(2)}) async-start(), calls=%async_computation.22 | async-start | bytes 1966080 | tf_op jit(solution)/shard_map/while/body/eval_jaxpr/all_gather | solution.py:112
  968.6 127.8 %all-gather.37.cloned.1.call-start = ((), (), s32[]{:S(2)}) async-start(), calls=%async_computation.25 | async-start | bytes 1216512 | tf_op jit(solution)/shard_map/while/body/eval_jaxpr/all_gather | solution.py:68
  969.4 192.3 %all-gather.39.cloned.1.call-start = ((), (), s32[]{:S(2)}) async-start(), calls=%async_computation.26 | async-start | bytes 4866048 | tf_op jit(solution)/shard_map/while/body/eval_jaxpr/all_gather | solution.py:72
  970.0 256.4 %all-gather.41.cloned.1.call-start = ((), (), s32[]{:S(2)}) async-start(), calls=%async_computation.27 | async-start | bytes 4866048 | tf_op jit(solution)/shard_map/while/body/eval_jaxpr/all_gather | solution.py:74
  970.7 333.1 %reduce-scatter.21.cloned.1.call-start = ((), (), s32[]{:S(2)}) async-start(), calls=%async_computation.28 | async-start | bytes 1966080 | tf_op jit(solution)/shard_map/while/body/eval_jaxpr/reduce_scatter | solution.py:237
  1266.1 70.6 %reduce-scatter.23.cloned.1.call-start = ((), (), s32[]{:S(2)}) async-start(), calls=%async_computation.29 | async-start | bytes 1966080 | tf_op jit(solution)/shard_map/while/body/eval_jaxpr/reduce_scatter | solution.py:243
  1345.3 56.5 %all-gather.33.cloned.1.call-start = ((), (), s32[]{:S(2)}) async-start(), calls=%async_computation.23 | async-start | bytes 1216512 | tf_op jit(solution)/shard_map/while/body/eval_jaxpr/all_gather | solution.py:66
  1345.8 111.4 %all-gather.29.cloned.1.call-start = ((), (), s32[]{:S(2)}) async-start(), calls=%async_computation.21 | async-start | bytes 1216512 | tf_op jit(solution)/shard_map/while/body/eval_jaxpr/all_gather | solution.py:65
  1346.6 148.1 %all-gather.35.cloned.1.call-start = ((), (), s32[]{:S(2)}) async-start(), calls=%async_computation.24 | async-start | bytes 1966080 | tf_op jit(solution)/shard_map/while/body/eval_jaxpr/all_gather | solution.py:113
  1404.3 127.7 %all-gather.31.cloned.1.call-start = ((), (), s32[]{:S(2)}) async-start(), calls=%async_computation.22 | async-start | bytes 1966080 | tf_op jit(solution)/shard_map/while/body/eval_jaxpr/all_gather | solution.py:112
  1459.8 127.8 %all-gather.37.cloned.1.call-start = ((), (), s32[]{:S(2)}) async-start(), calls=%async_computation.25 | async-start | bytes 1216512 | tf_op jit(solution)/shard_map/while/body/eval_jaxpr/all_gather | solution.py:68
  1460.6 192.4 %all-gather.39.cloned.1.call-start = ((), (), s32[]{:S(2)}) async-start(), calls=%async_computation.26 | async-start | bytes 4866048 | tf_op jit(solution)/shard_map/while/body/eval_jaxpr/all_gather | solution.py:72
  1461.3 256.3 %all-gather.41.cloned.1.call-start = ((), (), s32[]{:S(2)}) async-start(), calls=%async_computation.27 | async-start | bytes 4866048 | tf_op jit(solution)/shard_map/while/body/eval_jaxpr/all_gather | solution.py:74
  1461.9 339.9 %reduce-scatter.21.cloned.1.call-start = ((), (), s32[]{:S(2)}) async-start(), calls=%async_computation.28 | async-start | bytes 1966080 | tf_op jit(solution)/shard_map/while/body/eval_jaxpr/reduce_scatter | solution.py:237
  1757.4 70.6 %reduce-scatter.23.cloned.1.call-start = ((), (), s32[]{:S(2)}) async-start(), calls=%async_computation.29 | async-start | bytes 1966080 | tf_op jit(solution)/shard_map/while/body/eval_jaxpr/reduce_scatter | solution.py:243
  1838.7 104.8 %reduce-scatter.9.cloned.1.call-start = ((), (), s32[]{:S(2)}) async-start(), calls=%async_computation.8 | async-start | bytes 2433024 | tf_op jit(solution)/shard_map/reduce_scatter | solution.py:347
  1839.3 208.6 %reduce-scatter.11.cloned.1.call-start = ((), (), s32[]{:S(2)}) async-start(), calls=%async_computation.9 | async-start | bytes 2433024 | tf_op jit(solution)/shard_map/reduce_scatter | solution.py:347
  1839.9 312.3 %reduce-scatter.13.cloned.1.call-start = ((), (), s32[]{:S(2)}) async-start(), calls=%async_computation.10 | async-start | bytes 2433024 | tf_op jit(solution)/shard_map/reduce_scatter | solution.py:347
  1840.5 416.3 %reduce-scatter.15.cloned.1.call-start = ((), (), s32[]{:S(2)}) async-start(), calls=%async_computation.11 | async-start | bytes 2433024 | tf_op jit(solution)/shard_map/reduce_scatter | solution.py:347
  1841.2 557.3 %reduce-scatter.17.cloned.1.call-start = ((), (), s32[]{:S(2)}) async-start(), calls=%async_computation.12 | async-start | bytes 9732096 | tf_op jit(solution)/shard_map/reduce_scatter | solution.py:347
  1842.0 698.3 %reduce-scatter.19.cloned.1.call-start = ((), (), s32[]{:S(2)}) async-start(), calls=%async_computation.13 | async-start | bytes 9732096 | tf_op jit(solution)/shard_map/reduce_scatter | solution.py:347
  (143 other events, 2557.7 us)
Sparse Core Ops, SparseCore 0:
  57.9 55.9 all-gather.18
  116.7 53.1 all-gather.14
  172.0 35.9 all-gather.20
  210.0 35.8 all-gather.16
  248.5 52.8 all-gather.22
  304.1 62.5 all-gather.24
  369.4 61.8 all-gather.26
  447.9 52.6 all-gather.18
  503.4 52.8 all-gather.14
  558.2 35.9 all-gather.20
  596.4 35.8 all-gather.16
  635.0 52.8 all-gather.22
  690.6 62.5 all-gather.24
  755.8 61.8 all-gather.26
  857.8 52.4 all-gather.32
  913.0 53.0 all-gather.28
  967.4 35.9 all-gather.34
  1004.9 35.8 all-gather.30
  1043.6 52.8 all-gather.36
  1099.1 62.5 all-gather.38
  1164.5 61.8 all-gather.40
  1266.3 33.7 reduce-scatter.20
  1302.4 34.3 reduce-scatter.22
  1348.6 53.1 all-gather.32
  1404.5 52.6 all-gather.28
  1458.7 35.9 all-gather.34
  1496.1 35.8 all-gather.30
  1534.8 52.8 all-gather.36
  1590.5 62.5 all-gather.38
  1655.7 61.8 all-gather.40
  1757.5 33.7 reduce-scatter.20
  1793.5 34.3 reduce-scatter.22
Sparse Core Ops, SparseCore 1:
  1845.1 98.4 reduce-scatter.8
  1949.2 98.6 reduce-scatter.10
  2053.6 98.6 reduce-scatter.12
  2158.1 98.6 reduce-scatter.14
  2263.2 135.2 reduce-scatter.16
  2405.0 135.2 reduce-scatter.18
